TPU v7x, 256 devices: a whole 4x4x8 slice. The times are simulated.
256 devices in a mesh: head: 8 (over z), vocab: 32 (over y, x, core).
Axes of the slice: x: 4, y: 4, z: 8, core: 2. Of those that a mesh axis runs over, the one named last changes fastest.
Arguments:
- hidden_states: bfloat16 [2048, 8192], P(('head', 'vocab')), may hold values from -6 to 6
- head_weight: bfloat16 [8, 8192, 16384], P('head', None, 'vocab'), may hold values from -1 to 1
- tags: int32 [2048, 1], P(('head', 'vocab')), may hold values from 0 to 7; in each aligned block of 8 rows (0 to 7, 8 to 15, ...) at most 2 rows name the same one
- targets: int32 [2048], P(('head', 'vocab')), may hold values from 0 to 16383
- row_grad: bfloat16 [2048], P(('head', 'vocab')), may hold values from -192 to 192
Outputs:
- row_loss: bfloat16 [2048], P(('head', 'vocab'))
- hidden_grad: bfloat16 [2048, 8192], P(('head', 'vocab'))
Inputs may be any that keep to these rules, and one draw needn't show every extreme that they name: `tags`: in each aligned block of 8 rows (the rows of one device) no head is named by more than 2 rows, and in every draw some block has exactly 2 rows of one head.
All inputs are finite; a program needn't handle non-finite values.
Results may differ from a plain program's by a relative error of at most 0.018.
Values may be sent and summed in bfloat16 or wider, within the bound.
No kernel may reach another device: no remote copies, remote signals or barrier semaphores. Data moves between devices by JAX's collectives and lax.ppermute only.
A program may use at most 64 MiB of HBM per device.

v0:
```python
import jax
import jax.numpy as jnp
from jax import lax
from jax.sharding import PartitionSpec as P

CAP = 2


def project_back(dlog_block, weight):
    return lax.dot_general(
        dlog_block, weight, (((1,), (1,)), ((), ())), preferred_element_type=jnp.float32
    )


def per_device(hidden_states, head_weight, tags, targets, row_grad):
    head_count = lax.axis_size("head")
    own_rows = head_count * CAP
    row_tag = tags[:, 0]
    local_rows = row_tag.shape[0]
    row_iota = lax.broadcasted_iota(jnp.int32, (local_rows, local_rows), 0)
    col_iota = lax.broadcasted_iota(jnp.int32, (local_rows, local_rows), 1)
    earlier = (row_tag[None, :] == row_tag[:, None]) & (col_iota < row_iota)
    slot_rank = jnp.sum(earlier.astype(jnp.int32), axis=1)
    slot_index = row_tag * CAP + slot_rank
    selector = jnp.arange(own_rows, dtype=jnp.int32)[:, None] == slot_index[None, :]
    send_rows = jnp.dot(
        selector.astype(jnp.bfloat16), hidden_states, preferred_element_type=jnp.float32
    ).astype(jnp.bfloat16)
    send_rows = send_rows.reshape(head_count, CAP, hidden_states.shape[1])
    send_targets = jnp.sum(jnp.where(selector, targets[None, :], 0), axis=1).reshape(
        head_count, CAP
    )
    send_scale = (
        jnp.sum(jnp.where(selector, row_grad[None, :].astype(jnp.float32), 0.0), axis=1)
        .astype(jnp.bfloat16)
        .reshape(head_count, CAP)
    )
    arrived = (
        lax.all_to_all(send_rows, "head", split_axis=0, concat_axis=0, tiled=True),
        lax.all_to_all(send_targets, "head", split_axis=0, concat_axis=0, tiled=True),
        lax.all_to_all(send_scale, "head", split_axis=0, concat_axis=0, tiled=True),
    )
    grouped = (
        lax.all_gather(arrived[0], "vocab", axis=0, tiled=True),
        lax.all_gather(arrived[1], "vocab", axis=0, tiled=True),
        lax.all_gather(arrived[2], "vocab", axis=0, tiled=True),
    )
    gathered = grouped[0].reshape(-1, hidden_states.shape[1])
    group_targets = grouped[1].reshape(-1)
    group_scale = grouped[2].reshape(-1).astype(jnp.float32)
    weight = head_weight[0]
    vocab_width = weight.shape[1]
    logits = jnp.dot(gathered, weight, preferred_element_type=jnp.float32)
    offset = lax.axis_index("vocab") * vocab_width
    target_hit = lax.broadcasted_iota(jnp.int32, logits.shape, 1) + offset == group_targets[:, None]
    own_target = jnp.sum(jnp.where(target_hit, logits, 0.0), axis=1)
    row_top = lax.pmax(jnp.max(logits, axis=1), "vocab")
    local_total = jnp.sum(jnp.exp(logits - row_top[:, None]), axis=1)
    row_total, target_logit = lax.psum((local_total, own_target), "vocab")
    group_loss = (jnp.log(row_total) + row_top - target_logit).astype(jnp.bfloat16)
    probabilities = jnp.exp(logits - row_top[:, None]) / row_total[:, None]
    dlogits = (group_scale[:, None] * (probabilities - target_hit.astype(jnp.float32))).astype(
        jnp.bfloat16
    )
    partial_value = project_back(dlogits, weight)
    summed = lax.psum(partial_value.astype(jnp.bfloat16), "vocab").astype(jnp.float32)
    own_grad = lax.dynamic_slice_in_dim(summed, lax.axis_index("vocab") * own_rows, own_rows, 0)
    own_loss = lax.dynamic_slice_in_dim(group_loss, lax.axis_index("vocab") * own_rows, own_rows, 0)
    returned = (
        lax.all_to_all(
            own_grad.astype(jnp.bfloat16).reshape(head_count, CAP, -1),
            "head",
            split_axis=0,
            concat_axis=0,
            tiled=True,
        ),
        lax.all_to_all(
            own_loss.reshape(head_count, CAP), "head", split_axis=0, concat_axis=0, tiled=True
        ),
    )
    back_grad = returned[0].reshape(own_rows, -1)
    back_loss = returned[1].reshape(1, own_rows).astype(jnp.float32)
    hidden_grad = jnp.dot(
        selector.T.astype(jnp.bfloat16), back_grad, preferred_element_type=jnp.float32
    ).astype(jnp.bfloat16)
    row_loss = jnp.sum(jnp.where(selector.T, back_loss, 0.0), axis=1).astype(jnp.bfloat16)
    return (row_loss, hidden_grad)


def solution(mesh):
    placed = (
        P(("head", "vocab"), None),
        P("head", None, "vocab"),
        P(("head", "vocab"), None),
        P(("head", "vocab")),
        P(("head", "vocab")),
    )
    return jax.shard_map(
        per_device,
        mesh=mesh,
        in_specs=placed,
        out_specs=(P(("head", "vocab")), P(("head", "vocab"), None)),
        check_vma=False,
    )
```

profile of v0, /device:TPU:17, one launch (start us, length us, event | category | flops | bytes accessed | tf_op | source)
XLA Modules:
  0.0 415.1 jit_solution(14301299727951055076)
XLA Ops:
  7.2 0.9 convert_reduce_fusion.2
  9.3 18.6 %all_to_all.41 = bf16[8,2,8192]{2,1,0:T(2,128)(2,1)} all-to-all(bf16[8,2,8192]{2,1,0:T(2,128)(2,1)S(1)} %reshape.73), channel_id=1, replica_groups=mesh['head'=8,'vocab'=32] {'head'}, dimensions={0} | all-to-all | bytes 524288 | tf_op jit(solution)/shard_map/all_to_all | solution.py:39
  28.7 0.7 convert_element_type.91
  29.4 3.3 all-to-all-start.3
  32.7 0.7 select_reduce_fusion.2
  34.1 5.0 %all-to-all-done.3 = bf16[8,1,2]{2,1,0:T(2,128)(2,1)S(1)} async-done(((bf16[8,1,2]{2,1,0:T(2,128)(2,1)}), bf16[8,1,2]{2,1,0:T(2,128)(2,1)S(1)}, u32[]{:S(2)}, u32[]{:S(2)}) %all-to-all-start.3) | async-done | bytes 64 | tf_op jit(solution)/shard_map/all_to_all | solution.py:41
  39.2 3.3 all-to-all-start.1
  42.5 26.8 %all-gather.1 = bf16[256,1,2]{2,1,0:T(2,128)(2,1)S(1)} all-gather(bf16[8,1,2]{2,1,0:T(2,128)(2,1)S(1)} %all-to-all-done.3), channel_id=3, replica_groups=mesh['head'=8,'vocab'=32] {'vocab'}, dimensions={0}, use_global_device_ids=true | all-gather | bytes 1056 | tf_op jit(solution)/shard_map/all_gather | solution.py:46
  69.8 24.3 %all-gather = s32[256,1,2]{2,1,0:T(1,128)S(1)} all-gather(s32[8,1,2]{2,1,0:T(1,128)S(1)} %all-to-all-done.1), channel_id=2, replica_groups=mesh['head'=8,'vocab'=32] {'vocab'}, dimensions={0}, use_global_device_ids=true | all-gather | bytes 2112 | tf_op jit(solution)/shard_map/all_gather | solution.py:45
  94.7 1.0 reduce.11
  95.8 13.1 %reshape.74 = bf16[512,8192]{1,0:T(8,128)(2,1)} reshape(bf16[256,2,8192]{2,1,0:T(2,128)(2,1)} %all-gather.4.cloned.1.call-done) | data formatting | bytes 16777216 | tf_op jit(solution)/shard_map/reshape | solution.py:48
  108.9 11.0 %fusion.17 = (f32[512]{0:T(512)S(1)}, f32[512,512]{0,1:T(8,128)S(1)}) fusion(bf16[512,8192]{1,0:T(8,128)(2,1)} %reshape.74, bf16[1,8192,512]{2,1,0:T(8,128)(2,1)} %param.6), kind=kOutput, calls=%fused_computation.35 | convolution fusion | flops 4295228928 | bytes 17827840 | tf_op jit(solution)/shard_map/dot_general | solution.py:53
  119.9 52.5 %pmax.7 = f32[512]{0:T(512)S(1)} all-reduce(f32[512]{0:T(512)S(1)} %get-tuple-element.6), channel_id=1, replica_groups=mesh['head'=8,'vocab'=32] {'vocab'}, use_global_device_ids=true, to_apply=%region_2.3 | all-reduce | flops 512 | bytes 4096 | tf_op jit(solution)/shard_map/pmax | solution.py:57
  172.7 54.8 %all-reduce = (f32[512]{0:T(512)S(1)}, f32[512]{0:T(512)S(1)}) all-reduce(f32[512]{0:T(512)S(1)} %get-tuple-element.3, f32[512]{0:T(512)S(1)} %get-tuple-element.2), channel_id=1, replica_groups=mesh['head'=8,'vocab'=32] {'vocab'}, use_global_device_ids=true, to_apply=%region_7.8 | all-reduce | flops 1024 | bytes 8192 | tf_op jit(solution)/shard_map/psum | solution.py:59
  227.6 10.4 %convolution_convert_fusion = bf16[512,8192]{1,0:T(8,128)(2,1)} fusion(bf16[1,8192,512]{2,1,0:T(8,128)(2,1)} %param.6, f32[512,512]{0,1:T(8,128)S(1)} %get-tuple-element.7, f32[512]{0:T(512)S(1)} %get-tuple-element.5, f32[512]{0:T(512)S(1)} %reshape.78, s32[512]{0:T(512)S(1)} %eq.52, f32[512]{0:T(512)S(1)} %pmax.7, s32[512]{0:T(512)S(1)} %iota_add_fusion), kind=kOutput, calls=%fused_computation | convolution fusion | flops 4300996608 | bytes 17836032 | tf_op jit(solution)/shard_map/dot_general | solution.py:10
  238.1 0.7 all_to_all.35
  238.8 6.8 %all-to-all-start.2 = ((bf16[8,1,2]{2,1,0:T(2,128)(2,1)}), bf16[8,1,2]{2,1,0:T(2,128)(2,1)S(1)}, u32[]{:S(2)}, u32[]{:S(2)}) async-start(bf16[8,1,2]{2,1,0:T(2,128)(2,1)} %all_to_all.35), calls=%async_computation.2 | async-start | bytes 8192 | tf_op jit(solution)/shard_map/all_to_all | solution.py:77
  245.6 140.7 %all-reduce.3.cloned.1.call-done = bf16[512,8192]{1,0:T(8,128)(2,1)} async-done(((bf16[512,8192]{1,0:T(8,128)(2,1)}), bf16[512,8192]{1,0:T(8,128)(2,1)}) %all-reduce.3.cloned.1.call-update) | async-done | bytes 8388624 | tf_op jit(solution)/shard_map/psum | solution.py:66
  386.3 1.0 convert_convert_fusion
  387.2 0.9 reshape.75
  388.1 6.7 %all-to-all-start.4 = ((bf16[8,2,8192]{2,1,0:T(2,128)(2,1)}), bf16[8,2,8192]{2,1,0:T(2,128)(2,1)S(1)}, u32[]{:S(2)}, u32[]{:S(2)}) async-start(bf16[8,2,8192]{2,1,0:T(2,128)(2,1)} %reshape.75), calls=%async_computation.4 | async-start | bytes 524288 | tf_op jit(solution)/shard_map/all_to_all | solution.py:70
  395.0 0.7 select_reduce_fusion.1
  395.7 11.6 %all-to-all-done.4 = bf16[8,2,8192]{2,1,0:T(2,128)(2,1)S(1)} async-done(((bf16[8,2,8192]{2,1,0:T(2,128)(2,1)}), bf16[8,2,8192]{2,1,0:T(2,128)(2,1)S(1)}, u32[]{:S(2)}, u32[]{:S(2)}) %all-to-all-start.4) | async-done | bytes 262176 | tf_op jit(solution)/shard_map/all_to_all | solution.py:70
  407.4 0.9 convolution_convert_fusion.2
  (26 shorter events, 4.5 us)
Async XLA Ops:
  7.2 1.6 copy-start
  7.2 88.6 %all-gather.4.cloned.1.call-start = ((), (), s32[]{:S(2)}) async-start(), calls=%async_computation.5 | async-start | bytes 8650752 | tf_op jit(solution)/shard_map/all_gather | solution.py:44
  29.4 9.8 %all-to-all-start.3 = ((bf16[8,1,2]{2,1,0:T(2,128)(2,1)}), bf16[8,1,2]{2,1,0:T(2,128)(2,1)S(1)}, u32[]{:S(2)}, u32[]{:S(2)}) async-start(bf16[8,1,2]{2,1,0:T(2,128)(2,1)} %convert_element_type.91), calls=%async_computation.3 | async-start | bytes 8192 | tf_op jit(solution)/shard_map/all_to_all | solution.py:41
  39.2 30.7 %all-to-all-start.1 = ((s32[8,1,2]{2,1,0:T(1,128)}), s32[8,1,2]{2,1,0:T(1,128)S(1)}, u32[]{:S(2)}, u32[]{:S(2)}) async-start(s32[8,1,2]{2,1,0:T(1,128)} %bitcast.2), calls=%async_computation.1 | async-start | bytes 8192 | tf_op jit(solution)/shard_map/all_to_all | solution.py:40
  42.5 343.8 %all-reduce.3.cloned.1.call-start = ((), (), s32[]{:S(2)}) async-start(), calls=%async_computation.6 | async-start | bytes 16777216 | tf_op jit(solution)/shard_map/psum | solution.py:66
  238.8 149.3 %all-to-all-start.2 = ((bf16[8,1,2]{2,1,0:T(2,128)(2,1)}), bf16[8,1,2]{2,1,0:T(2,128)(2,1)S(1)}, u32[]{:S(2)}, u32[]{:S(2)}) async-start(bf16[8,1,2]{2,1,0:T(2,128)(2,1)} %all_to_all.35), calls=%async_computation.2 | async-start | bytes 8192 | tf_op jit(solution)/shard_map/all_to_all | solution.py:77
  388.1 19.1 %all-to-all-start.4 = ((bf16[8,2,8192]{2,1,0:T(2,128)(2,1)}), bf16[8,2,8192]{2,1,0:T(2,128)(2,1)S(1)}, u32[]{:S(2)}, u32[]{:S(2)}) async-start(bf16[8,2,8192]{2,1,0:T(2,128)(2,1)} %reshape.75), calls=%async_computation.4 | async-start | bytes 524288 | tf_op jit(solution)/shard_map/all_to_all | solution.py:70
Sparse Core Ops, SparseCore 0:
  28.1 56.0 all-gather.3
  238.1 148.1 all-reduce.2
where the time goes:
time: 416 us; the launch traced here: 415 us
  blocking collectives  177 us (43%)
  waiting for transfers between devices  157 us (38%)
  matrix products  22.7 us (5%)
  starting transfers between devices  20.2 us (5%)
  local copies, waits for them, and re-layouts  17.3 us (4%)
  between operations  14.2 us (3%)
  other arithmetic  6.38 us (2%)
    psum x1, waiting for transfers between devices, per_device(): lax.psum(partial_value.astype(jnp.bfloat16), 'vocab').astype(jnp.float32)  141 us
    psum x1, blocking collectives, per_device(): row_total, target_logit = lax.psum((local_total, own_target), 'vocab')  54.8 us
    pmax x1, blocking collectives, per_device(): row_top = lax.pmax(jnp.max(logits, axis=1), 'vocab')  52.5 us
    all_gather x1, blocking collectives, per_device(): lax.all_gather(arrived[2], 'vocab', axis=0, tiled=True)  26.8 us
    all_gather x1, blocking collectives, per_device(): lax.all_gather(arrived[1], 'vocab', axis=0, tiled=True)  24.3 us
    all_to_all x1, blocking collectives, per_device(): lax.all_to_all(send_rows, 'head', split_axis=0, concat_axis=0, tiled=True)  18.6 us
    reshape x1, local copies, waits for them, and re-layouts, per_device(): gathered = grouped[0].reshape(-1, hidden_states.shape[1])  13.1 us
    all_to_all x1, waiting for transfers between devices, per_device(): lax.all_to_all(own_grad.astype(jnp.bfloat16).reshape(head_count, CAP, -1)...  11.6 us
  transfers between devices with their start and end apart: 6, of which 3 were waited for; matrix products, arithmetic and copies ran while one was open for 2% of the time, Pallas kernels for 0%

commit v1 on v0

--- a/solution.py
+++ b/solution.py
@@ -4,6 +4,11 @@
 from jax.sharding import PartitionSpec as P
 
 CAP = 2
+
+
+def gather_over(shard, name, dim):
+    stack = jnp.stack([shard] * lax.axis_size(name))
+    return jnp.concatenate(lax.all_to_all(stack, name, 0, 0), axis=dim)
 
 
 def project_back(dlog_block, weight):
@@ -43,7 +48,7 @@
     grouped = (
         lax.all_gather(arrived[0], "vocab", axis=0, tiled=True),
         lax.all_gather(arrived[1], "vocab", axis=0, tiled=True),
-        lax.all_gather(arrived[2], "vocab", axis=0, tiled=True),
+        gather_over(arrived[2], "vocab", 0),
     )
     gathered = grouped[0].reshape(-1, hidden_states.shape[1])
     group_targets = grouped[1].reshape(-1)

time: 416 us -> 403 us (0.969)
  blocking collectives: 177 us -> 150 us
  starting transfers between devices: 20.2 us -> 28.3 us
  waiting for transfers between devices: 157 us -> 163 us
    all_gather x1 -> x0, blocking collectives: 26.8 us -> none  [per_device(): lax.all_gather(arrived[2], 'vocab', axis=0, tiled=True)]
    all_to_all x0 -> x1, starting transfers between devices: none -> 11.6 us  [gather_over(): return jnp.concatenate(lax.all_to_all(stack, name, 0, 0), axis=dim)]
    all_to_all x1, waiting for transfers between devices: 0.01 us -> 6.3 us  [per_device(): lax.all_to_all(send_targets, 'head', split_axis=0, concat_axis=0, tiled=T...]
  transfers between devices with their start and end apart: 6 -> 7, of which waited for: 3 -> 4; matrix products, arithmetic and copies ran while one was open for 2% -> 2% of each run, Pallas kernels for 0% -> 0%
where the time goes in v1:
time: 403 us
  waiting for transfers between devices  163 us (40%)
  blocking collectives  150 us (37%)
  starting transfers between devices  28.3 us (7%)
  matrix products  22.7 us (6%)
  local copies, waits for them, and re-layouts  18.2 us (5%)
  between operations  14.2 us (4%)
  other arithmetic  6 us (1%)
    psum x1, waiting for transfers between devices, per_device(): lax.psum(partial_value.astype(jnp.bfloat16), 'vocab').astype(jnp.float32)  140 us
    psum x1, blocking collectives, per_device(): row_total, target_logit = lax.psum((local_total, own_target), 'vocab')  54.9 us
    pmax x1, blocking collectives, per_device(): row_top = lax.pmax(jnp.max(logits, axis=1), 'vocab')  52.5 us
    all_gather x1, blocking collectives, per_device(): lax.all_gather(arrived[1], 'vocab', axis=0, tiled=True)  24 us
    all_to_all x1, blocking collectives, per_device(): lax.all_to_all(send_rows, 'head', split_axis=0, concat_axis=0, tiled=True)  18.6 us
    reshape x1, local copies, waits for them, and re-layouts, per_device(): gathered = grouped[0].reshape(-1, hidden_states.shape[1])  13.1 us
    all_to_all x1, starting transfers between devices, gather_over(): return jnp.concatenate(lax.all_to_all(stack, name, 0, 0), axis=dim)  11.6 us
    all_to_all x1, waiting for transfers between devices, per_device(): lax.all_to_all(own_grad.astype(jnp.bfloat16).reshape(head_count, CAP, -1)...  11.6 us
  transfers between devices with their start and end apart: 7, of which 4 were waited for; matrix products, arithmetic and copies ran while one was open for 2% of the time, Pallas kernels for 0%

profile of v1, /device:TPU:17, one launch (start us, length us, event | category | flops | bytes accessed | tf_op | source)
XLA Modules:
  0.0 402.6 jit_solution(208303824269343315)
XLA Ops:
  7.2 0.9 convert_reduce_fusion.1
  9.3 18.6 %all_to_all.43 = bf16[8,2,8192]{2,1,0:T(2,128)(2,1)} all-to-all(bf16[8,2,8192]{2,1,0:T(2,128)(2,1)S(1)} %reshape.75), channel_id=1, replica_groups=mesh['head'=8,'vocab'=32] {'head'}, dimensions={0} | all-to-all | bytes 524288 | tf_op jit(solution)/shard_map/all_to_all | solution.py:44
  28.7 0.7 convert_element_type.90
  29.4 3.3 all-to-all-start.3
  32.7 0.7 select_reduce_fusion.2
  34.1 5.1 %all-to-all-done.3 = bf16[8,1,2]{2,1,0:T(2,128)(2,1)S(1)} async-done(((bf16[8,1,2]{2,1,0:T(2,128)(2,1)}), bf16[8,1,2]{2,1,0:T(2,128)(2,1)S(1)}, u32[]{:S(2)}, u32[]{:S(2)}) %all-to-all-start.3) | async-done | bytes 64 | tf_op jit(solution)/shard_map/all_to_all | solution.py:46
  39.2 3.3 all-to-all-start.1
  42.6 6.3 %all-to-all-done.1 = s32[8,1,2]{2,1,0:T(1,128)S(1)} async-done(((s32[8,1,2]{2,1,0:T(1,128)}), s32[8,1,2]{2,1,0:T(1,128)S(1)}, u32[]{:S(2)}, u32[]{:S(2)}) %all-to-all-start.1) | async-done | bytes 96 | tf_op jit(solution)/shard_map/all_to_all | solution.py:45
  49.5 11.6 %all-to-all-start.4 = ((bf16[32,8,2]{1,2,0:T(2,128)(2,1)}), bf16[32,8,2]{1,2,0:T(2,128)(2,1)S(1)}, u32[]{:S(2)}, u32[]{:S(2)}) async-start(bf16[32,8,2]{1,2,0:T(2,128)(2,1)} %stack.5), calls=%async_computation.4 | async-start | bytes 32768 | tf_op jit(solution)/shard_map/all_to_all | solution.py:11
  61.2 24.0 %all-gather = s32[256,1,2]{2,1,0:T(1,128)S(1)} all-gather(s32[8,1,2]{2,1,0:T(1,128)S(1)} %all-to-all-done.1), channel_id=2, replica_groups=mesh['head'=8,'vocab'=32] {'vocab'}, dimensions={0}, use_global_device_ids=true | all-gather | bytes 2112 | tf_op jit(solution)/shard_map/all_gather | solution.py:50
  85.8 1.0 reduce.7
  87.3 13.1 %reshape.76 = bf16[512,8192]{1,0:T(8,128)(2,1)} reshape(bf16[256,2,8192]{2,1,0:T(2,128)(2,1)} %all-gather.3.cloned.1.call-done) | data formatting | bytes 16777216 | tf_op jit(solution)/shard_map/reshape | solution.py:53
  100.4 11.0 %fusion.17 = (f32[512]{0:T(512)S(1)}, f32[512,512]{0,1:T(8,128)S(1)}) fusion(bf16[512,8192]{1,0:T(8,128)(2,1)} %reshape.76, bf16[1,8192,512]{2,1,0:T(8,128)(2,1)} %param.6), kind=kOutput, calls=%fused_computation.34 | convolution fusion | flops 4295228928 | bytes 17827840 | tf_op jit(solution)/shard_map/dot_general | solution.py:58
  111.4 52.5 %pmax.7 = f32[512]{0:T(512)S(1)} all-reduce(f32[512]{0:T(512)S(1)} %get-tuple-element.6), channel_id=1, replica_groups=mesh['head'=8,'vocab'=32] {'vocab'}, use_global_device_ids=true, to_apply=%region_2.3 | all-reduce | flops 512 | bytes 4096 | tf_op jit(solution)/shard_map/pmax | solution.py:62
  164.2 54.9 %all-reduce = (f32[512]{0:T(512)S(1)}, f32[512]{0:T(512)S(1)}) all-reduce(f32[512]{0:T(512)S(1)} %get-tuple-element.3, f32[512]{0:T(512)S(1)} %get-tuple-element.2), channel_id=1, replica_groups=mesh['head'=8,'vocab'=32] {'vocab'}, use_global_device_ids=true, to_apply=%region_7.8 | all-reduce | flops 1024 | bytes 8192 | tf_op jit(solution)/shard_map/psum | solution.py:64
  219.1 10.4 %convolution_convert_fusion = bf16[512,8192]{1,0:T(8,128)(2,1)} fusion(bf16[1,8192,512]{2,1,0:T(8,128)(2,1)} %param.6, f32[512,512]{0,1:T(8,128)S(1)} %get-tuple-element.7, f32[512]{0:T(512)S(1)} %get-tuple-element.5, f32[512]{0:T(512)S(1)} %reshape.80, s32[512]{0:T(512)S(1)} %eq.52, f32[512]{0:T(512)S(1)} %pmax.7, s32[512]{0:T(512)S(1)} %iota_add_fusion), kind=kOutput, calls=%fused_computation | convolution fusion | flops 4300996608 | bytes 17836032 | tf_op jit(solution)/shard_map/dot_general | solution.py:15
  230.3 3.3 all-to-all-start.2
  233.7 140.1 %all-reduce.3.cloned.1.call-done = bf16[512,8192]{1,0:T(8,128)(2,1)} async-done(((bf16[512,8192]{1,0:T(8,128)(2,1)}), bf16[512,8192]{1,0:T(8,128)(2,1)}) %all-reduce.3.cloned.1.call-update) | async-done | bytes 8388624 | tf_op jit(solution)/shard_map/psum | solution.py:71
  373.8 1.0 convert_convert_fusion
  374.7 0.9 reshape.77
  375.6 6.7 %all-to-all-start.5 = ((bf16[8,2,8192]{2,1,0:T(2,128)(2,1)}), bf16[8,2,8192]{2,1,0:T(2,128)(2,1)S(1)}, u32[]{:S(2)}, u32[]{:S(2)}) async-start(bf16[8,2,8192]{2,1,0:T(2,128)(2,1)} %reshape.77), calls=%async_computation.5 | async-start | bytes 524288 | tf_op jit(solution)/shard_map/all_to_all | solution.py:75
  382.4 0.7 select_reduce_fusion.1
  383.1 11.6 %all-to-all-done.5 = bf16[8,2,8192]{2,1,0:T(2,128)(2,1)S(1)} async-done(((bf16[8,2,8192]{2,1,0:T(2,128)(2,1)}), bf16[8,2,8192]{2,1,0:T(2,128)(2,1)S(1)}, u32[]{:S(2)}, u32[]{:S(2)}) %all-to-all-start.5) | async-done | bytes 262176 | tf_op jit(solution)/shard_map/all_to_all | solution.py:75
  394.9 0.9 convolution_convert_fusion.2
  (30 shorter events, 5.7 us)
Async XLA Ops:
  7.2 1.6 copy-start
  7.2 80.1 %all-gather.3.cloned.1.call-start = ((), (), s32[]{:S(2)}) async-start(), calls=%async_computation.6 | async-start | bytes 8650752 | tf_op jit(solution)/shard_map/all_gather | solution.py:49
  29.4 9.8 %all-to-all-start.3 = ((bf16[8,1,2]{2,1,0:T(2,128)(2,1)}), bf16[8,1,2]{2,1,0:T(2,128)(2,1)S(1)}, u32[]{:S(2)}, u32[]{:S(2)}) async-start(bf16[8,1,2]{2,1,0:T(2,128)(2,1)} %convert_element_type.90), calls=%async_computation.3 | async-start | bytes 8192 | tf_op jit(solution)/shard_map/all_to_all | solution.py:46
  39.2 9.7 %all-to-all-start.1 = ((s32[8,1,2]{2,1,0:T(1,128)}), s32[8,1,2]{2,1,0:T(1,128)S(1)}, u32[]{:S(2)}, u32[]{:S(2)}) async-start(s32[8,1,2]{2,1,0:T(1,128)} %bitcast.2), calls=%async_computation.1 | async-start | bytes 8192 | tf_op jit(solution)/shard_map/all_to_all | solution.py:45
  49.5 37.4 %all-to-all-start.4 = ((bf16[32,8,2]{1,2,0:T(2,128)(2,1)}), bf16[32,8,2]{1,2,0:T(2,128)(2,1)S(1)}, u32[]{:S(2)}, u32[]{:S(2)}) async-start(bf16[32,8,2]{1,2,0:T(2,128)(2,1)} %stack.5), calls=%async_computation.4 | async-start | bytes 32768 | tf_op jit(solution)/shard_map/all_to_all | solution.py:11
  61.1 312.6 %all-reduce.3.cloned.1.call-start = ((), (), s32[]{:S(2)}) async-start(), calls=%async_computation.7 | async-start | bytes 16777216 | tf_op jit(solution)/shard_map/psum | solution.py:71
  230.3 145.3 %all-to-all-start.2 = ((bf16[8,1,2]{2,1,0:T(2,128)(2,1)}), bf16[8,1,2]{2,1,0:T(2,128)(2,1)S(1)}, u32[]{:S(2)}, u32[]{:S(2)}) async-start(bf16[8,1,2]{2,1,0:T(2,128)(2,1)} %all_to_all.36), calls=%async_computation.2 | async-start | bytes 8192 | tf_op jit(solution)/shard_map/all_to_all | solution.py:82
  375.6 19.1 %all-to-all-start.5 = ((bf16[8,2,8192]{2,1,0:T(2,128)(2,1)}), bf16[8,2,8192]{2,1,0:T(2,128)(2,1)S(1)}, u32[]{:S(2)}, u32[]{:S(2)}) async-start(bf16[8,2,8192]{2,1,0:T(2,128)(2,1)} %reshape.77), calls=%async_computation.5 | async-start | bytes 524288 | tf_op jit(solution)/shard_map/all_to_all | solution.py:75
Sparse Core Ops, SparseCore 0:
  28.1 56.3 all-gather.2
  229.7 144.0 all-reduce.2
